TPU v7x, 256 devices: a whole 4x4x8 slice. The times are simulated.
256 devices in a mesh: grp: 32 (over z, y_hi, core), tp: 8 (over y_lo, x).
Axes of the slice: x: 4, y: 4 (y_hi: 2, y_lo: 2; y = y_hi * 2 + y_lo), z: 8, core: 2. Of those that a mesh axis runs over, the one named last changes fastest.
Arguments:
- states_in: bfloat16 [16384, 1536], P('grp', 'tp'), may hold values from -6 to 6
- segment_ids: int32 [16384], P('grp'), may hold values from 0 to 223, as said below
- positions: int32 [16384], P('grp'), may hold values from 0 to 1009, as said below
- attention_gain: bfloat16 [1536], P('tp'), may hold values from 0.5 to 1.5
- feedforward_gain: bfloat16 [1536], P('tp'), may hold values from 0.5 to 1.5
- query_weight: bfloat16 [1536, 1536], P('grp', 'tp'), may hold values from -1 to 1
- keyvalue_weight: bfloat16 [1536, 8, 128], P('grp', 'tp'), may hold values from -128 to 128
- output_weight: bfloat16 [1536, 1536], P('tp'), may hold values from -0.15625 to 0.15625
- route_experts: int32 [16384, 8], P('grp'), may hold values from 0 to 19, all different within a row; in each aligned block of 512 rows (0 to 511, 512 to 1023, ...) at most 256 rows name the same one
- route_weights: float32 [16384, 8], P('grp'), may hold values from 0.05 to 0.3
- expert_gateup: bfloat16 [40, 1536, 512], P('tp'), may hold values from -0.15625 to 0.15625
- expert_down: bfloat16 [40, 256, 1536], P('tp'), may hold values from -0.25 to 0.25
- cache_slots: int32 [16384], P('grp'), may hold values from 0 to 16383, as said below
Outputs:
- layer_output: bfloat16 [16384, 1536], P('grp', 'tp')
- paged_cache: bfloat16 [16384, 8, 128], P('grp', 'tp')
- log_sums: float32 [24, 16384], P('tp', 'grp')
Inputs may be any that keep to these rules, and one draw needn't show every extreme that they name: `segment_ids`: equal ids mark the tokens of one prompt; the tokens of a prompt lie within one pair of groups 2p and 2p+1. `positions`: positions count from 0 within each prompt; one prompt of groups 0 and 1 has 2 * (505) tokens. `route_experts`: each row names 8 different experts; at most 256 rows of one group name the same expert, and that number is reached. `cache_slots`: every cache row is named once; the tokens of each group fill exactly 16 rows of every group's block of 512 rows.
All inputs are finite; a program needn't handle non-finite values.
Results may differ from a plain program's by a relative error of at most 0.01.
The roundings to bfloat16 on the way count: a program that leaves them out, or rounds other values in their place, can miss the bound.
Values may be sent and summed in bfloat16 or wider, within the bound.
No kernel may reach another device: no remote copies, remote signals or barrier semaphores. Data moves between devices by JAX's collectives and lax.ppermute only.
A program may use at most 128 MiB of HBM per device.

v0:
```python
import jax
import jax.numpy as jnp
from jax import lax
from jax.sharding import Mesh
from jax.sharding import PartitionSpec as P

HD = 64
attn_scale = 0.015625
norm_eps = 1e-06
rope_base = 10000.0
G = ("z", "yh", "c")
T = ("yl", "x")


def rms_scale(values, gain_row):
    floats = values.astype(jnp.float32)
    mean_square = jnp.mean(floats * floats, axis=-1, keepdims=True)
    return (floats * lax.rsqrt(mean_square + norm_eps) * gain_row.astype(jnp.float32)).astype(
        jnp.bfloat16
    )


def rotate(values, places):
    half_width = values.shape[-1] // 2
    frequency = rope_base ** (-jnp.arange(half_width, dtype=jnp.float32) * 2.0 / values.shape[-1])
    angles = places.astype(jnp.float32)[:, None] * frequency[None, :]
    cosine = jnp.cos(angles)[:, None, :]
    sine_part = jnp.sin(angles)[:, None, :]
    leading = values[..., :half_width]
    trailing = values[..., half_width:]
    return jnp.concatenate(
        [leading * cosine - trailing * sine_part, trailing * cosine + leading * sine_part], axis=-1
    )


def attend_block(query_block, seg_block, pos_block, all_rows, all_seg, all_pos):
    key_part = all_rows[..., :HD]
    value_part = all_rows[..., HD:]
    scores = (
        jnp.einsum("qgrd,kgd->grqk", query_block, key_part, preferred_element_type=jnp.float32)
        * attn_scale
    )
    allowed = (seg_block[:, None] == all_seg[None, :]) & (all_pos[None, :] <= pos_block[:, None])
    masked = jnp.where(allowed, scores, -jnp.inf)
    row_peak = jnp.max(masked, axis=-1, keepdims=True)
    exponent = jnp.exp(masked - row_peak)
    row_total = jnp.sum(exponent, axis=-1, keepdims=True)
    log_total = (row_peak + jnp.log(row_total))[..., 0]
    weights_low = (exponent / row_total).astype(jnp.bfloat16)
    mixed_rows = jnp.einsum(
        "grqk,kgd->qgrd", weights_low, value_part, preferred_element_type=jnp.float32
    )
    return (mixed_rows.astype(jnp.bfloat16), log_total)


def expert_terms(normed, route_experts, route_weights, gateup, down, slot_first):
    local_experts = gateup.shape[0]
    half_units = down.shape[1]
    owned_experts = slot_first + jnp.arange(local_experts, dtype=jnp.int32)
    matches = route_experts[:, :, None] == owned_experts[None, None, :]
    route_scale = jnp.sum(jnp.where(matches, route_weights[:, :, None], 0.0), axis=1)
    gate_up = jnp.einsum("td,edf->etf", normed, gateup, preferred_element_type=jnp.float32)
    activated = (jax.nn.silu(gate_up[..., :half_units]) * gate_up[..., half_units:]).astype(
        jnp.bfloat16
    )
    produced = jnp.einsum("etf,efd->etd", activated, down, preferred_element_type=jnp.float32)
    return jnp.sum(route_scale.T[:, :, None] * produced, axis=0)


def gather_rows_over_groups(block):
    width = block.shape[1]
    ci = lax.axis_index("c")
    other_c = lax.ppermute(block, "c", [(0, 1), (1, 0)])
    cfull = jnp.where(ci == 0, jnp.stack([block, other_c]), jnp.stack([other_c, block]))
    yi = lax.axis_index("yh")
    other_y = lax.ppermute(cfull, "yh", [(0, 1), (1, 0)])
    yfull = jnp.where(yi == 0, jnp.stack([cfull, other_y]), jnp.stack([other_y, cfull]))
    nz = lax.axis_size("z")
    zi = lax.axis_index("z")
    got = [yfull]
    for k in range(1, nz):
        got.append(lax.ppermute(yfull, "z", [(i, (i + k) % nz) for i in range(nz)]))
    stacked = jnp.stack(got)
    zfull = jnp.take(stacked, (zi - jnp.arange(nz)) % nz, axis=0)
    return zfull.reshape(-1, width)


def place_cache_rows(own_rows, cache_slots, group_rank):
    tokens, keyvalue_heads, row_width = own_rows.shape
    width = keyvalue_heads * row_width
    group_count = lax.axis_size(G)
    per_owner = tokens // group_count
    sequence = jnp.arange(tokens, dtype=jnp.int32)
    owners = cache_slots // tokens
    owner_hot = (owners[:, None] == jnp.arange(group_count, dtype=jnp.int32)[None, :]).astype(
        jnp.bfloat16
    )
    earlier = (sequence[:, None] > sequence[None, :]).astype(jnp.bfloat16)
    before = jnp.dot(earlier, owner_hot, preferred_element_type=jnp.float32)
    rank = jnp.sum(before * owner_hot.astype(jnp.float32), axis=1).astype(jnp.int32)
    place = owners * per_owner + rank
    moving = (place[None, :] == sequence[:, None]).astype(jnp.bfloat16)
    digits = jnp.stack([cache_slots // 128, cache_slots % 128], axis=1).astype(jnp.bfloat16)
    payload = jnp.concatenate([own_rows.reshape(tokens, width), digits], axis=1)
    sent = jnp.dot(moving, payload, preferred_element_type=jnp.float32).astype(jnp.bfloat16)
    sent_rows = sent[:, :width].reshape(group_count, per_owner, width)
    sent_digits = sent[:, width:].reshape(group_count, per_owner, 2).transpose(0, 2, 1)
    digit_row = jnp.zeros((group_count, 1, width), jnp.bfloat16)
    digit_row = lax.dynamic_update_slice(
        digit_row, sent_digits.reshape(group_count, 1, 2 * per_owner), (0, 0, 0)
    )
    packet = jnp.concatenate([sent_rows, digit_row], axis=1)
    got = lax.all_to_all(packet, G, 0, 0, tiled=True)
    got_rows = got[:, :per_owner, :].reshape(tokens, width)
    got_digits = (
        got[:, per_owner, : 2 * per_owner].astype(jnp.int32).reshape(group_count, 2, per_owner)
    )
    got_slots = (got_digits[:, 0, :] * 128 + got_digits[:, 1, :]).reshape(tokens)
    targets = got_slots - group_rank * tokens
    landing = (targets[None, :] == sequence[:, None]).astype(jnp.bfloat16)
    placed = jnp.dot(landing, got_rows, preferred_element_type=jnp.float32).astype(jnp.bfloat16)
    return placed.reshape(tokens, keyvalue_heads, row_width)


def shards(
    states_in,
    segment_ids,
    positions,
    attention_gain,
    feedforward_gain,
    query_weight,
    keyvalue_weight,
    output_weight,
    route_experts,
    route_weights,
    expert_gateup,
    expert_down,
    cache_slots,
):
    tokens = states_in.shape[0]
    width_share = states_in.shape[1]
    head_rank = lax.axis_index(T)
    group_rank = lax.axis_index(G)
    gain_rows = jnp.zeros((8, width_share), states_in.dtype)
    gain_rows = gain_rows.at[0].set(attention_gain).at[1].set(feedforward_gain)
    packed = jnp.concatenate([states_in, gain_rows], axis=0)
    packed_full = lax.all_gather(packed, T, axis=1, tiled=True)
    states_full = packed_full[:tokens]
    gain_attend = packed_full[tokens]
    gain_forward = packed_full[tokens + 1]
    normed_in = rms_scale(states_full, gain_attend)
    query_cols = query_weight.shape[1]
    keyvalue_heads = keyvalue_weight.shape[1]
    heads_local = query_cols // HD
    piece_rows = query_weight.shape[0]
    weights_packed = jnp.concatenate(
        [query_weight, keyvalue_weight.reshape(piece_rows, -1)], axis=1
    )
    weights_full = gather_rows_over_groups(weights_packed)
    query_full_w = weights_full[:, :query_cols]
    keyvalue_full_w = weights_full[:, query_cols:]
    query_sum = jnp.dot(normed_in, query_full_w, preferred_element_type=jnp.float32)
    keyvalue_sum = jnp.dot(normed_in, keyvalue_full_w, preferred_element_type=jnp.float32)
    queries = rotate(query_sum.reshape(tokens, heads_local, HD), positions).astype(jnp.bfloat16)
    keyvalue_sum = keyvalue_sum.reshape(tokens, keyvalue_heads, 2 * HD)
    key_rows = rotate(keyvalue_sum[..., :HD], positions).astype(jnp.bfloat16)
    value_rows = keyvalue_sum[..., HD:].astype(jnp.bfloat16)
    own_rows = jnp.concatenate([key_rows, value_rows], axis=-1)
    other_rows, other_seg, other_pos = lax.ppermute(
        (own_rows, segment_ids, positions), "c", [(0, 1), (1, 0)]
    )
    all_rows = jnp.concatenate([own_rows, other_rows], axis=0)
    all_seg = jnp.concatenate([segment_ids, other_seg], axis=0)
    all_pos = jnp.concatenate([positions, other_pos], axis=0)
    group_ratio = heads_local // keyvalue_heads
    query_block = queries.reshape(tokens, keyvalue_heads, group_ratio, HD)
    mixed, log_part = attend_block(query_block, segment_ids, positions, all_rows, all_seg, all_pos)
    attended = mixed.reshape(tokens, heads_local * HD)
    log_sums = log_part.reshape(heads_local, tokens)
    partial_value = jnp.dot(attended, output_weight, preferred_element_type=jnp.float32)
    tp_count = lax.axis_size(T)
    value_parts = (
        partial_value.astype(jnp.bfloat16).reshape(tokens, tp_count, width_share).transpose(1, 0, 2)
    )
    value_got = lax.all_to_all(value_parts, T, 0, 0, tiled=True)
    summed_share = jnp.sum(value_got.astype(jnp.float32), axis=0)
    residual_share = (states_in.astype(jnp.float32) + summed_share).astype(jnp.bfloat16)
    residual_share, own_rows, cache_slots = lax.optimization_barrier(
        (residual_share, own_rows, cache_slots)
    )
    residual = lax.all_gather(residual_share, T, axis=1, tiled=True)
    paged_rows = place_cache_rows(own_rows, cache_slots, group_rank)
    residual, paged_rows = lax.optimization_barrier((residual, paged_rows))
    normed = rms_scale(residual, gain_forward)
    slot_first = head_rank // 2 * expert_gateup.shape[0]
    terms = expert_terms(
        normed, route_experts, route_weights, expert_gateup, expert_down, slot_first
    )
    term_parts = (
        terms.astype(jnp.bfloat16).reshape(tokens, tp_count, width_share).transpose(1, 0, 2)
    )
    term_got = lax.all_to_all(term_parts, T, 0, 0, tiled=True)
    expert_share = jnp.sum(term_got.astype(jnp.float32), axis=0)
    layer_output = (residual_share.astype(jnp.float32) + expert_share).astype(jnp.bfloat16)
    return (layer_output, paged_rows, log_sums)


def solution(mesh):
    fine = Mesh(mesh.devices.reshape(8, 2, 2, 2, 4), ("z", "yh", "c", "yl", "x"))
    return jax.shard_map(
        shards,
        mesh=fine,
        in_specs=(
            P(G, T),
            P(G),
            P(G),
            P(T),
            P(T),
            P(G, T),
            P(G, T, None),
            P(T, None),
            P(G, None),
            P(G, None),
            P(T, None, None),
            P(T, None, None),
            P(G),
        ),
        out_specs=(P(G, T), P(G, T, None), P(T, G)),
        check_vma=False,
    )
```

profile of v0, /device:TPU:32, one launch (start us, length us, event | category | flops | bytes accessed | tf_op | source)
XLA Modules:
  0.0 187.5 jit_solution(6620179228807870160)
XLA Ops:
  9.7 1.7 pad_maximum_fusion.1
  15.4 1.5 compare_and_fusion
  17.0 3.3 %collective-permute-start.1 = (bf16[2,48,320]{2,1,0:T(8,128)(2,1)S(1)}, bf16[2,48,320]{2,1,0:T(8,128)(2,1)S(1)}, u32[]{:S(2)}, u32[]{:S(2)}) collective-permute-start(bf16[2,48,320]{2,1,0:T(8,128)(2,1)S(1)} %maximum_select_fusion.3), channel_id=1, source_target_pairs={{0,16},{16,0},{1,17},{17,1},{2,18},{18,2},{3,19},{19,3},{4,20},{20... | collective-permute-start | bytes 184328 | tf_op jit(solution)/shard_map/ppermute | solution.py:76
  20.3 2.9 %collective-permute-done.1 = bf16[2,48,320]{2,1,0:T(8,128)(2,1)S(1)} collective-permute-done((bf16[2,48,320]{2,1,0:T(8,128)(2,1)S(1)}, bf16[2,48,320]{2,1,0:T(8,128)(2,1)S(1)}, u32[]{:S(2)}, u32[]{:S(2)}) %collective-permute-start.1) | collective-permute-done | bytes 61472 | tf_op jit(solution)/shard_map/ppermute | solution.py:76
  23.2 2.0 %collective-permute-start.2 = (bf16[2,2,48,320]{3,2,1,0:T(8,128)(2,1)S(1)}, bf16[2,2,48,320]{3,2,1,0:T(8,128)(2,1)S(1)}, u32[]{:S(2)}, u32[]{:S(2)}) collective-permute-start(bf16[2,2,48,320]{3,2,1,0:T(8,128)(2,1)S(1)} %maximum_select_fusion.1), channel_id=1, source_target_pairs={{0,32},{32,64},{64,96},{96,128},{128,160},{160,192},{192,224},{224... | collective-permute-start | bytes 368648 | tf_op jit(solution)/shard_map/ppermute | solution.py:82
  25.2 4.6 %collective-permute-start.3 = (bf16[2,2,48,320]{3,2,1,0:T(8,128)(2,1)S(1)}, bf16[2,2,48,320]{3,2,1,0:T(8,128)(2,1)S(1)}, u32[]{:S(2)}, u32[]{:S(2)}) collective-permute-start(bf16[2,2,48,320]{3,2,1,0:T(8,128)(2,1)S(1)} %maximum_select_fusion.1), channel_id=1, source_target_pairs={{0,64},{32,96},{64,128},{96,160},{128,192},{160,224},{192,0},{224,... | collective-permute-start | bytes 368648 | tf_op jit(solution)/shard_map/ppermute | solution.py:82
  29.8 1.9 %collective-permute-start.4 = (bf16[2,2,48,320]{3,2,1,0:T(8,128)(2,1)S(1)}, bf16[2,2,48,320]{3,2,1,0:T(8,128)(2,1)S(1)}, u32[]{:S(2)}, u32[]{:S(2)}) collective-permute-start(bf16[2,2,48,320]{3,2,1,0:T(8,128)(2,1)S(1)} %maximum_select_fusion.1), channel_id=1, source_target_pairs={{0,96},{32,128},{64,160},{96,192},{128,224},{160,0},{192,32},{224,... | collective-permute-start | bytes 368648 | tf_op jit(solution)/shard_map/ppermute | solution.py:82
  31.7 1.4 collective-permute-start.5
  33.2 3.0 %collective-permute-start.6 = (bf16[2,2,48,320]{3,2,1,0:T(8,128)(2,1)S(1)}, bf16[2,2,48,320]{3,2,1,0:T(8,128)(2,1)S(1)}, u32[]{:S(2)}, u32[]{:S(2)}) collective-permute-start(bf16[2,2,48,320]{3,2,1,0:T(8,128)(2,1)S(1)} %maximum_select_fusion.1), channel_id=1, source_target_pairs={{0,160},{32,192},{64,224},{96,0},{128,32},{160,64},{192,96},{224,1... | collective-permute-start | bytes 368648 | tf_op jit(solution)/shard_map/ppermute | solution.py:82
  36.3 2.5 %collective-permute-start.7 = (bf16[2,2,48,320]{3,2,1,0:T(8,128)(2,1)S(1)}, bf16[2,2,48,320]{3,2,1,0:T(8,128)(2,1)S(1)}, u32[]{:S(2)}, u32[]{:S(2)}) collective-permute-start(bf16[2,2,48,320]{3,2,1,0:T(8,128)(2,1)S(1)} %maximum_select_fusion.1), channel_id=1, source_target_pairs={{0,192},{32,224},{64,0},{96,32},{128,64},{160,96},{192,128},{224,1... | collective-permute-start | bytes 368648 | tf_op jit(solution)/shard_map/ppermute | solution.py:82
  38.8 1.2 collective-permute-done.3
  40.1 3.8 %collective-permute-start.8 = (bf16[2,2,48,320]{3,2,1,0:T(8,128)(2,1)S(1)}, bf16[2,2,48,320]{3,2,1,0:T(8,128)(2,1)S(1)}, u32[]{:S(2)}, u32[]{:S(2)}) collective-permute-start(bf16[2,2,48,320]{3,2,1,0:T(8,128)(2,1)S(1)} %maximum_select_fusion.1), channel_id=1, source_target_pairs={{0,224},{32,0},{64,32},{96,64},{128,96},{160,128},{192,160},{224,1... | collective-permute-start | bytes 368648 | tf_op jit(solution)/shard_map/ppermute | solution.py:82
  43.9 9.9 %collective-permute-done.4 = bf16[2,2,48,320]{3,2,1,0:T(8,128)(2,1)S(1)} collective-permute-done((bf16[2,2,48,320]{3,2,1,0:T(8,128)(2,1)S(1)}, bf16[2,2,48,320]{3,2,1,0:T(8,128)(2,1)S(1)}, u32[]{:S(2)}, u32[]{:S(2)}) %collective-permute-start.4) | collective-permute-done | bytes 122912 | tf_op jit(solution)/shard_map/ppermute | solution.py:82
  54.0 6.0 %collective-permute-done.7 = bf16[2,2,48,320]{3,2,1,0:T(8,128)(2,1)S(1)} collective-permute-done((bf16[2,2,48,320]{3,2,1,0:T(8,128)(2,1)S(1)}, bf16[2,2,48,320]{3,2,1,0:T(8,128)(2,1)S(1)}, u32[]{:S(2)}, u32[]{:S(2)}) %collective-permute-start.7) | collective-permute-done | bytes 122912 | tf_op jit(solution)/shard_map/ppermute | solution.py:82
  60.0 1.5 collective-permute-done.8
  62.7 1.9 %fusion.2 = f32[512]{0:T(512)S(1)} fusion(bf16[520,1536]{0,1:T(8,128)(2,1)} %all-gather.3.cloned.1.call-done), kind=kLoop, calls=%fused_computation.11 | loop fusion | flops 2358784 | bytes 1574912 | tf_op jit(solution)/shard_map/reduce_sum | solution.py:17
  64.6 1.5 convert_reduce_fusion.2
  69.1 1.4 fusion.1
  70.5 1.4 fusion
  71.9 2.0 %fusion.17 = bf16[64,3,512]{2,0,1:T(8,128)(2,1)S(1)} fusion(f32[3,512]{1,0:T(4,128)S(1)} %fusion, f32[3,512]{1,0:T(4,128)S(1)} %get-tuple-element.51, f32[1024,512,3]{1,0,2:T(8,128)S(1)} %get-tuple-element.52, pred[512,1024]{0,1:T(8,128)(4,1)S(1)} %compare_and_fusion, bf16[1024,1,128]{0,2,1:T(8,128)(2,1)S(1)} %pad_maximum_fusion), kind=kOutput, calls=%fused_computation.31 | convolution fusion | flops 209289216 | bytes 7159808 | tf_op jit(solution)/shard_map/grqk,kgd->qgrd/dot_general | solution.py:50
  74.5 1.6 copy.67
  76.1 27.0 %all_to_all.15 = bf16[8,512,192]{1,2,0:T(8,128)(2,1)S(1)} all-to-all(bf16[8,512,192]{1,2,0:T(8,128)(2,1)} %bitcast.96), channel_id=1, replica_groups=mesh['z'=8,'yh'=2,'c'=2,'yl'=2,'x'=4] {'yl','x'}, dimensions={0} | all-to-all | bytes 3145728 | tf_op jit(solution)/shard_map/all_to_all | solution.py:185
  106.0 6.6 %all-to-all-start.1 = ((bf16[32,17,128]{2,1,0:T(8,128)(2,1)}), bf16[32,17,128]{2,1,0:T(8,128)(2,1)S(1)}, u32[]{:S(2)}, u32[]{:S(2)}) async-start(bf16[32,17,128]{2,1,0:T(8,128)(2,1)} %fusion.30), calls=%async_computation.1 | async-start | bytes 393216 | tf_op jit(solution)/shard_map/all_to_all | solution.py:113
  112.7 11.6 %all-to-all-done.1 = bf16[32,17,128]{2,1,0:T(8,128)(2,1)S(1)} async-done(((bf16[32,17,128]{2,1,0:T(8,128)(2,1)}), bf16[32,17,128]{2,1,0:T(8,128)(2,1)S(1)}, u32[]{:S(2)}, u32[]{:S(2)}) %all-to-all-start.1) | async-done | bytes 139296 | tf_op jit(solution)/shard_map/all_to_all | solution.py:113
  124.6 1.0 fusion.20
  125.6 17.9 %all-gather.5.cloned.1.call-done = bf16[512,1536]{0,1:T(8,128)(2,1)} async-done(((bf16[512,192]{0,1:T(8,128)(2,1)}), bf16[512,1536]{0,1:T(8,128)(2,1)}) %all-gather.5.cloned.1.call-update) | async-done | bytes 1572880 | tf_op jit(solution)/shard_map/all_gather | solution.py:191
  143.5 1.8 fusion.5
  145.3 8.7 %convolution_bitcast_fusion = f32[5,512,512]{2,1,0:T(8,128)S(1)} fusion(bf16[5,1536,512]{2,1,0:T(8,128)(2,1)} %param.27, bf16[512,1536]{0,1:T(8,128)(2,1)} %all-gather.5.cloned.1.call-done, f32[1536]{0:T(1024)S(1)} %get-tuple-element.37, f32[512]{0:T(512)S(1)} %add_rsqrt_fusion), kind=kOutput, calls=%fused_computation.24 | convolution fusion | flops 4029677568 | bytes 14688256 | tf_op jit(solution)/shard_map/td,edf->etf/dot_general | solution.py:62
  154.0 3.5 %multiply_reduce_fusion = bf16[512,1536]{1,0:T(8,128)(2,1)S(1)} fusion(bf16[5,256,1536]{2,1,0:T(8,128)(2,1)S(1)} %copy-done.8, f32[5,512]{1,0:T(8,128)S(1)} %bitcast.110, f32[5,512,512]{2,1,0:T(8,128)S(1)} %convolution_bitcast_fusion), kind=kOutput, calls=%fused_computation.1 | convolution fusion | flops 2024275968 | bytes 10758144 | tf_op jit(solution)/shard_map/etf,efd->etd/dot_general | solution.py:66
  157.5 1.6 copy.75
  159.1 3.7 %all-to-all-start.2 = ((bf16[8,512,192]{1,2,0:T(8,128)(2,1)}), bf16[8,512,192]{1,2,0:T(8,128)(2,1)S(1)}, u32[]{:S(2)}, u32[]{:S(2)}) async-start(bf16[8,512,192]{1,2,0:T(8,128)(2,1)} %bitcast.42), calls=%async_computation.2 | async-start | bytes 3145728 | tf_op jit(solution)/shard_map/all_to_all | solution.py:202
  163.4 16.3 %all-to-all-done.2 = bf16[8,512,192]{1,2,0:T(8,128)(2,1)S(1)} async-done(((bf16[8,512,192]{1,2,0:T(8,128)(2,1)}), bf16[8,512,192]{1,2,0:T(8,128)(2,1)S(1)}, u32[]{:S(2)}, u32[]{:S(2)}) %all-to-all-start.2) | async-done | bytes 1572896 | tf_op jit(solution)/shard_map/all_to_all | solution.py:202
  (101 shorter events, 16.2 us)
Async XLA Ops:
  7.2 66.7 %copy-start = (bf16[192,1536]{1,0:T(8,128)(2,1)S(1)}, bf16[192,1536]{1,0:T(8,128)(2,1)}, u32[]{:S(2)}) copy-start(bf16[192,1536]{1,0:T(8,128)(2,1)} %param.24) | copy-start | bytes 1769476
  7.2 55.5 %all-gather.3.cloned.1.call-start = ((), (), s32[]{:S(2)}) async-start(), calls=%async_computation.3 | async-start | bytes 2211840 | tf_op jit(solution)/shard_map/all_gather | solution.py:147
  8.1 8.8 %collective-permute-start = (bf16[48,320]{1,0:T(8,128)(2,1)S(1)}, bf16[48,320]{1,0:T(8,128)(2,1)S(1)}, u32[]{:S(2)}, u32[]{:S(2)}) collective-permute-start(bf16[48,320]{1,0:T(8,128)(2,1)S(1)} %get-tuple-element.45), channel_id=1, source_target_pairs={{0,8},{8,0},{1,9},{9,1},{2,10},{10,2},{3,11},{11,3},{4,12},{12,4},... | collective-permute-start | bytes 92168 | tf_op jit(solution)/shard_map/ppermute | solution.py:73
  11.4 132.0 %all-gather.5.cloned.1.call-start = ((), (), s32[]{:S(2)}) async-start(), calls=%async_computation.4 | async-start | bytes 1769472 | tf_op jit(solution)/shard_map/all_gather | solution.py:191
  11.5 2.5 %collective-permute-start.10 = (s32[512]{0:T(512)}, s32[512]{0:T(512)S(1)}, u32[]{:S(2)}, u32[]{:S(2)}) collective-permute-start(s32[512]{0:T(512)} %param.18), channel_id=1, source_target_pairs={{0,8},{8,0},{1,9},{9,1},{2,10},{10,2},{3,11},{11,3},{4,12},{12,4},... | collective-permute-start | bytes 6152 | tf_op jit(solution)/shard_map/ppermute | solution.py:169
  12.1 2.7 %collective-permute-start.11 = (s32[512]{0:T(512)}, s32[512]{0:T(512)S(1)}, u32[]{:S(2)}, u32[]{:S(2)}) collective-permute-start(s32[512]{0:T(512)} %param.19), channel_id=1, source_target_pairs={{0,8},{8,0},{1,9},{9,1},{2,10},{10,2},{3,11},{11,3},{4,12},{12,4},... | collective-permute-start | bytes 6152 | tf_op jit(solution)/shard_map/ppermute | solution.py:169
  17.0 6.2 %collective-permute-start.1 = (bf16[2,48,320]{2,1,0:T(8,128)(2,1)S(1)}, bf16[2,48,320]{2,1,0:T(8,128)(2,1)S(1)}, u32[]{:S(2)}, u32[]{:S(2)}) collective-permute-start(bf16[2,48,320]{2,1,0:T(8,128)(2,1)S(1)} %maximum_select_fusion.3), channel_id=1, source_target_pairs={{0,16},{16,0},{1,17},{17,1},{2,18},{18,2},{3,19},{19,3},{4,20},{20... | collective-permute-start | bytes 184328 | tf_op jit(solution)/shard_map/ppermute | solution.py:76
  23.2 13.0 %collective-permute-start.2 = (bf16[2,2,48,320]{3,2,1,0:T(8,128)(2,1)S(1)}, bf16[2,2,48,320]{3,2,1,0:T(8,128)(2,1)S(1)}, u32[]{:S(2)}, u32[]{:S(2)}) collective-permute-start(bf16[2,2,48,320]{3,2,1,0:T(8,128)(2,1)S(1)} %maximum_select_fusion.1), channel_id=1, source_target_pairs={{0,32},{32,64},{64,96},{96,128},{128,160},{160,192},{192,224},{224... | collective-permute-start | bytes 368648 | tf_op jit(solution)/shard_map/ppermute | solution.py:82
  25.2 14.8 %collective-permute-start.3 = (bf16[2,2,48,320]{3,2,1,0:T(8,128)(2,1)S(1)}, bf16[2,2,48,320]{3,2,1,0:T(8,128)(2,1)S(1)}, u32[]{:S(2)}, u32[]{:S(2)}) collective-permute-start(bf16[2,2,48,320]{3,2,1,0:T(8,128)(2,1)S(1)} %maximum_select_fusion.1), channel_id=1, source_target_pairs={{0,64},{32,96},{64,128},{96,160},{128,192},{160,224},{192,0},{224,... | collective-permute-start | bytes 368648 | tf_op jit(solution)/shard_map/ppermute | solution.py:82
  29.8 24.0 %collective-permute-start.4 = (bf16[2,2,48,320]{3,2,1,0:T(8,128)(2,1)S(1)}, bf16[2,2,48,320]{3,2,1,0:T(8,128)(2,1)S(1)}, u32[]{:S(2)}, u32[]{:S(2)}) collective-permute-start(bf16[2,2,48,320]{3,2,1,0:T(8,128)(2,1)S(1)} %maximum_select_fusion.1), channel_id=1, source_target_pairs={{0,96},{32,128},{64,160},{96,192},{128,224},{160,0},{192,32},{224,... | collective-permute-start | bytes 368648 | tf_op jit(solution)/shard_map/ppermute | solution.py:82
  31.7 22.2 %collective-permute-start.5 = (bf16[2,2,48,320]{3,2,1,0:T(8,128)(2,1)S(1)}, bf16[2,2,48,320]{3,2,1,0:T(8,128)(2,1)S(1)}, u32[]{:S(2)}, u32[]{:S(2)}) collective-permute-start(bf16[2,2,48,320]{3,2,1,0:T(8,128)(2,1)S(1)} %maximum_select_fusion.1), channel_id=1, source_target_pairs={{0,128},{32,160},{64,192},{96,224},{128,0},{160,32},{192,64},{224,... | collective-permute-start | bytes 368648 | tf_op jit(solution)/shard_map/ppermute | solution.py:82
  33.2 20.8 %collective-permute-start.6 = (bf16[2,2,48,320]{3,2,1,0:T(8,128)(2,1)S(1)}, bf16[2,2,48,320]{3,2,1,0:T(8,128)(2,1)S(1)}, u32[]{:S(2)}, u32[]{:S(2)}) collective-permute-start(bf16[2,2,48,320]{3,2,1,0:T(8,128)(2,1)S(1)} %maximum_select_fusion.1), channel_id=1, source_target_pairs={{0,160},{32,192},{64,224},{96,0},{128,32},{160,64},{192,96},{224,1... | collective-permute-start | bytes 368648 | tf_op jit(solution)/shard_map/ppermute | solution.py:82
  36.3 23.7 %collective-permute-start.7 = (bf16[2,2,48,320]{3,2,1,0:T(8,128)(2,1)S(1)}, bf16[2,2,48,320]{3,2,1,0:T(8,128)(2,1)S(1)}, u32[]{:S(2)}, u32[]{:S(2)}) collective-permute-start(bf16[2,2,48,320]{3,2,1,0:T(8,128)(2,1)S(1)} %maximum_select_fusion.1), channel_id=1, source_target_pairs={{0,192},{32,224},{64,0},{96,32},{128,64},{160,96},{192,128},{224,1... | collective-permute-start | bytes 368648 | tf_op jit(solution)/shard_map/ppermute | solution.py:82
  40.1 21.4 %collective-permute-start.8 = (bf16[2,2,48,320]{3,2,1,0:T(8,128)(2,1)S(1)}, bf16[2,2,48,320]{3,2,1,0:T(8,128)(2,1)S(1)}, u32[]{:S(2)}, u32[]{:S(2)}) collective-permute-start(bf16[2,2,48,320]{3,2,1,0:T(8,128)(2,1)S(1)} %maximum_select_fusion.1), channel_id=1, source_target_pairs={{0,224},{32,0},{64,32},{96,64},{128,96},{160,128},{192,160},{224,1... | collective-permute-start | bytes 368648 | tf_op jit(solution)/shard_map/ppermute | solution.py:82
  62.7 3.5 %copy-start.1 = (bf16[520,1536]{0,1:T(8,128)(2,1)S(1)}, bf16[520,1536]{0,1:T(8,128)(2,1)}, u32[]{:S(2)}) copy-start(bf16[520,1536]{0,1:T(8,128)(2,1)} %all-gather.3.cloned.1.call-done) | copy-start | bytes 4792324
  67.4 1.1 copy-start.4
  67.5 1.6 collective-permute-start.9
  76.1 27.2 %copy-start.3 = (bf16[512,192]{0,1:T(8,128)(2,1)S(1)}, bf16[512,192]{0,1:T(8,128)(2,1)}, u32[]{:S(2)}) copy-start(bf16[512,192]{0,1:T(8,128)(2,1)} %param.17) | copy-start | bytes 589828
  103.1 1.0 copy-start.7
  103.4 9.2 %copy-start.5 = (f32[512,8]{0,1:T(8,128)S(1)}, f32[512,8]{0,1:T(8,128)}, u32[]{:S(2)}) copy-start(f32[512,8]{0,1:T(8,128)} %param.26) | copy-start | bytes 49156
  103.4 9.2 %copy-start.6 = (s32[512,8]{0,1:T(8,128)S(1)}, s32[512,8]{0,1:T(8,128)}, u32[]{:S(2)}) copy-start(s32[512,8]{0,1:T(8,128)} %param.25) | copy-start | bytes 49156
  106.0 18.4 %all-to-all-start.1 = ((bf16[32,17,128]{2,1,0:T(8,128)(2,1)}), bf16[32,17,128]{2,1,0:T(8,128)(2,1)S(1)}, u32[]{:S(2)}, u32[]{:S(2)}) async-start(bf16[32,17,128]{2,1,0:T(8,128)(2,1)} %fusion.30), calls=%async_computation.1 | async-start | bytes 393216 | tf_op jit(solution)/shard_map/all_to_all | solution.py:113
  145.3 8.7 %copy-start.8 = (bf16[5,256,1536]{2,1,0:T(8,128)(2,1)S(1)}, bf16[5,256,1536]{2,1,0:T(8,128)(2,1)}, u32[]{:S(2)}) copy-start(bf16[5,256,1536]{2,1,0:T(8,128)(2,1)} %param.28) | copy-start | bytes 11796484
  159.1 20.9 %copy-start.2 = (bf16[512,192]{0,1:T(8,128)(2,1)S(1)}, bf16[512,192]{0,1:T(8,128)(2,1)}, u32[]{:S(2)}) copy-start(bf16[512,192]{0,1:T(8,128)(2,1)} %add_convert_fusion.1) | copy-start | bytes 589828
  159.1 20.6 %all-to-all-start.2 = ((bf16[8,512,192]{1,2,0:T(8,128)(2,1)}), bf16[8,512,192]{1,2,0:T(8,128)(2,1)S(1)}, u32[]{:S(2)}, u32[]{:S(2)}) async-start(bf16[8,512,192]{1,2,0:T(8,128)(2,1)} %bitcast.42), calls=%async_computation.2 | async-start | bytes 3145728 | tf_op jit(solution)/shard_map/all_to_all | solution.py:202
Sparse Core Ops, SparseCore 0:
  11.5 46.6 all-gather.2
  104.2 39.1 all-gather.4
where the time goes:
time: 188 us
  waiting for transfers between devices  67.8 us (36%)
  starting transfers between devices  34.1 us (18%)
  blocking collectives  27 us (14%)
  matrix products  19.5 us (10%)
  other arithmetic  18.1 us (10%)
  between operations  14.6 us (8%)
  local copies, waits for them, and re-layouts  6.55 us (3%)
    all_to_all x1, blocking collectives, shards(): value_got = lax.all_to_all(value_parts, T, 0, 0, tiled=True)  27 us
    ppermute x7, starting transfers between devices, gather_rows_over_groups(): got.append(lax.ppermute(yfull, 'z', [(i, (i + k) % nz) for i in range(nz)]))  19.3 us
    ppermute x7, waiting for transfers between devices, gather_rows_over_groups(): got.append(lax.ppermute(yfull, 'z', [(i, (i + k) % nz) for i in range(nz)]))  18.6 us
    all_gather x1, waiting for transfers between devices, shards(): residual = lax.all_gather(residual_share, T, axis=1, tiled=True)  17.9 us
    all_to_all x1, waiting for transfers between devices, shards(): term_got = lax.all_to_all(term_parts, T, 0, 0, tiled=True)  16.3 us
    all_to_all x1, waiting for transfers between devices, place_cache_rows(): got = lax.all_to_all(packet, G, 0, 0, tiled=True)  11.6 us
    dot_general x1, matrix products, expert_terms(): jnp.einsum('td,edf->etf', normed, gateup, preferred_element_type=jnp.floa...  8.71 us
    all_to_all x1, starting transfers between devices, place_cache_rows(): got = lax.all_to_all(packet, G, 0, 0, tiled=True)  6.58 us
  transfers between devices with their start and end apart: 16, of which 9 were waited for; matrix products, arithmetic and copies ran while one was open for 7% of the time, Pallas kernels for 0%

commit v1 on v0

--- a/solution.py
+++ b/solution.py
@@ -188,7 +188,9 @@
     residual_share, own_rows, cache_slots = lax.optimization_barrier(
         (residual_share, own_rows, cache_slots)
     )
-    residual = lax.all_gather(residual_share, T, axis=1, tiled=True)
+    residual = jnp.concatenate(
+        lax.all_to_all(jnp.stack([residual_share] * lax.axis_size(T)), T, 0, 0), axis=1
+    )
     paged_rows = place_cache_rows(own_rows, cache_slots, group_rank)
     residual, paged_rows = lax.optimization_barrier((residual, paged_rows))
     normed = rms_scale(residual, gain_forward)

time: 188 us -> 199 us (1.059); the launches traced: 188 us -> 195 us
  blocking collectives: 27 us -> 45.1 us
  waiting for transfers between devices: 67.8 us -> 61.8 us
  starting transfers between devices: 34.1 us -> 31.1 us
  other arithmetic: 18.1 us -> 15.5 us
    all_to_all x0 -> x1, blocking collectives: none -> 18 us  [place_cache_rows(): got = lax.all_to_all(packet, G, 0, 0, tiled=True)]
    all_gather x1 -> x0, waiting for transfers between devices: 17.9 us -> none  [shards(): residual = lax.all_gather(residual_share, T, axis=1, tiled=True)]
    all_to_all x1, waiting for transfers between devices: 11.6 us -> 19.1 us  [shards(): lax.all_to_all(jnp.stack([residual_share] * lax.axis_size(T)), T, 0, 0)]
    all_to_all x1, waiting for transfers between devices: 16.3 us -> 20.8 us  [shards(): term_got = lax.all_to_all(term_parts, T, 0, 0, tiled=True)]
    all_to_all x1, starting transfers between devices: 6.58 us -> 3.8 us  [shards(): lax.all_to_all(jnp.stack([residual_share] * lax.axis_size(T)), T, 0, 0)]
  transfers between devices with their start and end apart: 16 -> 15, of which waited for: 9 -> 8; matrix products, arithmetic and copies ran while one was open for 7% -> 6% of each run, Pallas kernels for 0% -> 0%
where the time goes in v1:
time: 199 us; the launch traced here: 195 us
  waiting for transfers between devices  61.8 us (31%)
  blocking collectives  45.1 us (23%)
  starting transfers between devices  31.1 us (16%)
  matrix products  19 us (10%)
  other arithmetic  15.5 us (8%)
  between operations  14.6 us (7%)
  local copies, waits for them, and re-layouts  8.23 us (4%)
    all_to_all x1, blocking collectives, shards(): value_got = lax.all_to_all(value_parts, T, 0, 0, tiled=True)  27.1 us
    all_to_all x1, waiting for transfers between devices, shards(): term_got = lax.all_to_all(term_parts, T, 0, 0, tiled=True)  20.8 us
    ppermute x7, starting transfers between devices, gather_rows_over_groups(): got.append(lax.ppermute(yfull, 'z', [(i, (i + k) % nz) for i in range(nz)]))  19.3 us
    all_to_all x1, waiting for transfers between devices, shards(): lax.all_to_all(jnp.stack([residual_share] * lax.axis_size(T)), T, 0, 0)  19.1 us
    ppermute x7, waiting for transfers between devices, gather_rows_over_groups(): got.append(lax.ppermute(yfull, 'z', [(i, (i + k) % nz) for i in range(nz)]))  18.6 us
    all_to_all x1, blocking collectives, place_cache_rows(): got = lax.all_to_all(packet, G, 0, 0, tiled=True)  18 us
    dot_general x1, matrix products, expert_terms(): jnp.einsum('td,edf->etf', normed, gateup, preferred_element_type=jnp.floa...  8.29 us
  transfers between devices with their start and end apart: 15, of which 8 were waited for; matrix products, arithmetic and copies ran while one was open for 6% of the time, Pallas kernels for 0%

profile of v1, /device:TPU:32, one launch (start us, length us, event | category | flops | bytes accessed | tf_op | source)
XLA Modules:
  0.0 195.3 jit_solution(6806177817256361713)
XLA Ops:
  9.7 1.7 pad_maximum_fusion.1
  15.4 1.5 compare_and_fusion
  16.9 3.3 %collective-permute-start.1 = (bf16[2,48,320]{2,1,0:T(8,128)(2,1)S(1)}, bf16[2,48,320]{2,1,0:T(8,128)(2,1)S(1)}, u32[]{:S(2)}, u32[]{:S(2)}) collective-permute-start(bf16[2,48,320]{2,1,0:T(8,128)(2,1)S(1)} %maximum_select_fusion.3), channel_id=1, source_target_pairs={{0,16},{16,0},{1,17},{17,1},{2,18},{18,2},{3,19},{19,3},{4,20},{20... | collective-permute-start | bytes 184328 | tf_op jit(solution)/shard_map/ppermute | solution.py:76
  20.2 2.9 %collective-permute-done.1 = bf16[2,48,320]{2,1,0:T(8,128)(2,1)S(1)} collective-permute-done((bf16[2,48,320]{2,1,0:T(8,128)(2,1)S(1)}, bf16[2,48,320]{2,1,0:T(8,128)(2,1)S(1)}, u32[]{:S(2)}, u32[]{:S(2)}) %collective-permute-start.1) | collective-permute-done | bytes 61472 | tf_op jit(solution)/shard_map/ppermute | solution.py:76
  23.2 2.0 %collective-permute-start.2 = (bf16[2,2,48,320]{3,2,1,0:T(8,128)(2,1)S(1)}, bf16[2,2,48,320]{3,2,1,0:T(8,128)(2,1)S(1)}, u32[]{:S(2)}, u32[]{:S(2)}) collective-permute-start(bf16[2,2,48,320]{3,2,1,0:T(8,128)(2,1)S(1)} %maximum_select_fusion.1), channel_id=1, source_target_pairs={{0,32},{32,64},{64,96},{96,128},{128,160},{160,192},{192,224},{224... | collective-permute-start | bytes 368648 | tf_op jit(solution)/shard_map/ppermute | solution.py:82
  25.2 4.6 %collective-permute-start.3 = (bf16[2,2,48,320]{3,2,1,0:T(8,128)(2,1)S(1)}, bf16[2,2,48,320]{3,2,1,0:T(8,128)(2,1)S(1)}, u32[]{:S(2)}, u32[]{:S(2)}) collective-permute-start(bf16[2,2,48,320]{3,2,1,0:T(8,128)(2,1)S(1)} %maximum_select_fusion.1), channel_id=1, source_target_pairs={{0,64},{32,96},{64,128},{96,160},{128,192},{160,224},{192,0},{224,... | collective-permute-start | bytes 368648 | tf_op jit(solution)/shard_map/ppermute | solution.py:82
  29.8 1.9 collective-permute-start.4
  31.7 1.4 collective-permute-start.5
  33.1 3.0 %collective-permute-start.6 = (bf16[2,2,48,320]{3,2,1,0:T(8,128)(2,1)S(1)}, bf16[2,2,48,320]{3,2,1,0:T(8,128)(2,1)S(1)}, u32[]{:S(2)}, u32[]{:S(2)}) collective-permute-start(bf16[2,2,48,320]{3,2,1,0:T(8,128)(2,1)S(1)} %maximum_select_fusion.1), channel_id=1, source_target_pairs={{0,160},{32,192},{64,224},{96,0},{128,32},{160,64},{192,96},{224,1... | collective-permute-start | bytes 368648 | tf_op jit(solution)/shard_map/ppermute | solution.py:82
  36.2 2.5 %collective-permute-start.7 = (bf16[2,2,48,320]{3,2,1,0:T(8,128)(2,1)S(1)}, bf16[2,2,48,320]{3,2,1,0:T(8,128)(2,1)S(1)}, u32[]{:S(2)}, u32[]{:S(2)}) collective-permute-start(bf16[2,2,48,320]{3,2,1,0:T(8,128)(2,1)S(1)} %maximum_select_fusion.1), channel_id=1, source_target_pairs={{0,192},{32,224},{64,0},{96,32},{128,64},{160,96},{192,128},{224,1... | collective-permute-start | bytes 368648 | tf_op jit(solution)/shard_map/ppermute | solution.py:82
  38.8 1.2 collective-permute-done.3
  40.0 3.8 %collective-permute-start.8 = (bf16[2,2,48,320]{3,2,1,0:T(8,128)(2,1)S(1)}, bf16[2,2,48,320]{3,2,1,0:T(8,128)(2,1)S(1)}, u32[]{:S(2)}, u32[]{:S(2)}) collective-permute-start(bf16[2,2,48,320]{3,2,1,0:T(8,128)(2,1)S(1)} %maximum_select_fusion.1), channel_id=1, source_target_pairs={{0,224},{32,0},{64,32},{96,64},{128,96},{160,128},{192,160},{224,1... | collective-permute-start | bytes 368648 | tf_op jit(solution)/shard_map/ppermute | solution.py:82
  43.9 9.9 %collective-permute-done.4 = bf16[2,2,48,320]{3,2,1,0:T(8,128)(2,1)S(1)} collective-permute-done((bf16[2,2,48,320]{3,2,1,0:T(8,128)(2,1)S(1)}, bf16[2,2,48,320]{3,2,1,0:T(8,128)(2,1)S(1)}, u32[]{:S(2)}, u32[]{:S(2)}) %collective-permute-start.4) | collective-permute-done | bytes 122912 | tf_op jit(solution)/shard_map/ppermute | solution.py:82
  53.9 6.0 %collective-permute-done.7 = bf16[2,2,48,320]{3,2,1,0:T(8,128)(2,1)S(1)} collective-permute-done((bf16[2,2,48,320]{3,2,1,0:T(8,128)(2,1)S(1)}, bf16[2,2,48,320]{3,2,1,0:T(8,128)(2,1)S(1)}, u32[]{:S(2)}, u32[]{:S(2)}) %collective-permute-start.7) | collective-permute-done | bytes 122912 | tf_op jit(solution)/shard_map/ppermute | solution.py:82
  59.9 1.5 collective-permute-done.8
  62.6 1.9 fusion.2
  64.6 1.7 convert_reduce_fusion.2
  69.2 1.3 fusion.1
  70.5 1.4 fusion
  71.9 2.0 %fusion.17 = bf16[64,3,512]{2,0,1:T(8,128)(2,1)S(1)} fusion(f32[3,512]{1,0:T(4,128)S(1)} %fusion, f32[3,512]{1,0:T(4,128)S(1)} %get-tuple-element.51, f32[1024,512,3]{1,0,2:T(8,128)S(1)} %get-tuple-element.52, pred[512,1024]{0,1:T(8,128)(4,1)S(1)} %compare_and_fusion, bf16[1024,1,128]{0,2,1:T(8,128)(2,1)S(1)} %pad_maximum_fusion), kind=kOutput, calls=%fused_computation.31 | convolution fusion | flops 209289216 | bytes 7159808 | tf_op jit(solution)/shard_map/grqk,kgd->qgrd/dot_general | solution.py:50
  74.6 1.6 copy.67
  76.2 27.1 %all_to_all.20 = bf16[8,512,192]{1,2,0:T(8,128)(2,1)S(1)} all-to-all(bf16[8,512,192]{1,2,0:T(8,128)(2,1)} %bitcast.101), channel_id=1, replica_groups=mesh['z'=8,'yh'=2,'c'=2,'yl'=2,'x'=4] {'yl','x'}, dimensions={0} | all-to-all | bytes 3145728 | tf_op jit(solution)/shard_map/all_to_all | solution.py:185
  105.1 18.0 %all_to_all.21 = bf16[32,17,128]{2,1,0:T(8,128)(2,1)S(1)} all-to-all(bf16[32,17,128]{2,1,0:T(8,128)(2,1)S(1)} %fusion.30), channel_id=1, replica_groups=mesh['z'=8,'yh'=2,'c'=2,'yl'=2,'x'=4] {'z','yh','c'}, dimensions={0} | all-to-all | bytes 278528 | tf_op jit(solution)/shard_map/all_to_all | solution.py:113
  123.1 1.3 stack.111
  124.4 3.8 %all-to-all-start.1 = ((bf16[8,512,192]{1,2,0:T(8,128)(2,1)}), bf16[8,512,192]{1,2,0:T(8,128)(2,1)S(1)}, u32[]{:S(2)}, u32[]{:S(2)}) async-start(bf16[8,512,192]{1,2,0:T(8,128)(2,1)} %stack.111), calls=%async_computation.1 | async-start | bytes 3145728 | tf_op jit(solution)/shard_map/all_to_all | solution.py:192
  128.7 1.0 fusion.20
  129.7 19.1 %all-to-all-done.1 = bf16[8,512,192]{1,2,0:T(8,128)(2,1)S(1)} async-done(((bf16[8,512,192]{1,2,0:T(8,128)(2,1)}), bf16[8,512,192]{1,2,0:T(8,128)(2,1)S(1)}, u32[]{:S(2)}, u32[]{:S(2)}) %all-to-all-start.1) | async-done | bytes 1572896 | tf_op jit(solution)/shard_map/all_to_all | solution.py:192
  149.2 8.3 %convolution_bitcast_fusion = f32[5,512,512]{2,1,0:T(8,128)S(1)} fusion(bf16[5,1536,512]{2,1,0:T(8,128)(2,1)} %param.27, bf16[512,1536]{0,1:T(8,128)(2,1)S(1)} %bitcast.100, f32[1536]{0:T(1024)S(1)} %get-tuple-element.37, f32[512]{0:T(512)S(1)} %add_rsqrt_fusion), kind=kOutput, calls=%fused_computation.24 | convolution fusion | flops 4029677568 | bytes 14688256 | tf_op jit(solution)/shard_map/td,edf->etf/dot_general | solution.py:62
  157.5 3.5 %multiply_reduce_fusion = bf16[512,1536]{1,0:T(8,128)(2,1)S(1)} fusion(bf16[5,256,1536]{2,1,0:T(8,128)(2,1)S(1)} %copy-done.9, f32[5,512]{1,0:T(8,128)S(1)} %bitcast.115, f32[5,512,512]{2,1,0:T(8,128)S(1)} %convolution_bitcast_fusion), kind=kOutput, calls=%fused_computation.1 | convolution fusion | flops 2024275968 | bytes 10758144 | tf_op jit(solution)/shard_map/etf,efd->etd/dot_general | solution.py:66
  161.0 1.6 copy.75
  162.6 3.6 %all-to-all-start.3 = ((bf16[8,512,192]{1,2,0:T(8,128)(2,1)}), bf16[8,512,192]{1,2,0:T(8,128)(2,1)S(1)}, u32[]{:S(2)}, u32[]{:S(2)}) async-start(bf16[8,512,192]{1,2,0:T(8,128)(2,1)} %bitcast.44), calls=%async_computation.3 | async-start | bytes 3145728 | tf_op jit(solution)/shard_map/all_to_all | solution.py:204
  166.8 20.8 %all-to-all-done.3 = bf16[8,512,192]{1,2,0:T(8,128)(2,1)S(1)} async-done(((bf16[8,512,192]{1,2,0:T(8,128)(2,1)}), bf16[8,512,192]{1,2,0:T(8,128)(2,1)S(1)}, u32[]{:S(2)}, u32[]{:S(2)}) %all-to-all-start.3) | async-done | bytes 1572896 | tf_op jit(solution)/shard_map/all_to_all | solution.py:204
  (102 shorter events, 15.5 us)
Async XLA Ops:
  7.2 66.8 %copy-start = (bf16[192,1536]{1,0:T(8,128)(2,1)S(1)}, bf16[192,1536]{1,0:T(8,128)(2,1)}, u32[]{:S(2)}) copy-start(bf16[192,1536]{1,0:T(8,128)(2,1)} %param.24) | copy-start | bytes 1769476
  7.2 55.4 %all-gather.2.cloned.1.call-start = ((), (), s32[]{:S(2)}) async-start(), calls=%async_computation.4 | async-start | bytes 2211840 | tf_op jit(solution)/shard_map/all_gather | solution.py:147
  8.1 8.8 %collective-permute-start = (bf16[48,320]{1,0:T(8,128)(2,1)S(1)}, bf16[48,320]{1,0:T(8,128)(2,1)S(1)}, u32[]{:S(2)}, u32[]{:S(2)}) collective-permute-start(bf16[48,320]{1,0:T(8,128)(2,1)S(1)} %get-tuple-element.45), channel_id=1, source_target_pairs={{0,8},{8,0},{1,9},{9,1},{2,10},{10,2},{3,11},{11,3},{4,12},{12,4},... | collective-permute-start | bytes 92168 | tf_op jit(solution)/shard_map/ppermute | solution.py:73
  11.4 2.5 %collective-permute-start.10 = (s32[512]{0:T(512)}, s32[512]{0:T(512)S(1)}, u32[]{:S(2)}, u32[]{:S(2)}) collective-permute-start(s32[512]{0:T(512)} %param.18), channel_id=1, source_target_pairs={{0,8},{8,0},{1,9},{9,1},{2,10},{10,2},{3,11},{11,3},{4,12},{12,4},... | collective-permute-start | bytes 6152 | tf_op jit(solution)/shard_map/ppermute | solution.py:169
  12.0 2.7 %collective-permute-start.11 = (s32[512]{0:T(512)}, s32[512]{0:T(512)S(1)}, u32[]{:S(2)}, u32[]{:S(2)}) collective-permute-start(s32[512]{0:T(512)} %param.19), channel_id=1, source_target_pairs={{0,8},{8,0},{1,9},{9,1},{2,10},{10,2},{3,11},{11,3},{4,12},{12,4},... | collective-permute-start | bytes 6152 | tf_op jit(solution)/shard_map/ppermute | solution.py:169
  16.9 6.2 %collective-permute-start.1 = (bf16[2,48,320]{2,1,0:T(8,128)(2,1)S(1)}, bf16[2,48,320]{2,1,0:T(8,128)(2,1)S(1)}, u32[]{:S(2)}, u32[]{:S(2)}) collective-permute-start(bf16[2,48,320]{2,1,0:T(8,128)(2,1)S(1)} %maximum_select_fusion.3), channel_id=1, source_target_pairs={{0,16},{16,0},{1,17},{17,1},{2,18},{18,2},{3,19},{19,3},{4,20},{20... | collective-permute-start | bytes 184328 | tf_op jit(solution)/shard_map/ppermute | solution.py:76
  23.2 13.0 %collective-permute-start.2 = (bf16[2,2,48,320]{3,2,1,0:T(8,128)(2,1)S(1)}, bf16[2,2,48,320]{3,2,1,0:T(8,128)(2,1)S(1)}, u32[]{:S(2)}, u32[]{:S(2)}) collective-permute-start(bf16[2,2,48,320]{3,2,1,0:T(8,128)(2,1)S(1)} %maximum_select_fusion.1), channel_id=1, source_target_pairs={{0,32},{32,64},{64,96},{96,128},{128,160},{160,192},{192,224},{224... | collective-permute-start | bytes 368648 | tf_op jit(solution)/shard_map/ppermute | solution.py:82
  25.2 14.8 %collective-permute-start.3 = (bf16[2,2,48,320]{3,2,1,0:T(8,128)(2,1)S(1)}, bf16[2,2,48,320]{3,2,1,0:T(8,128)(2,1)S(1)}, u32[]{:S(2)}, u32[]{:S(2)}) collective-permute-start(bf16[2,2,48,320]{3,2,1,0:T(8,128)(2,1)S(1)} %maximum_select_fusion.1), channel_id=1, source_target_pairs={{0,64},{32,96},{64,128},{96,160},{128,192},{160,224},{192,0},{224,... | collective-permute-start | bytes 368648 | tf_op jit(solution)/shard_map/ppermute | solution.py:82
  29.8 24.0 %collective-permute-start.4 = (bf16[2,2,48,320]{3,2,1,0:T(8,128)(2,1)S(1)}, bf16[2,2,48,320]{3,2,1,0:T(8,128)(2,1)S(1)}, u32[]{:S(2)}, u32[]{:S(2)}) collective-permute-start(bf16[2,2,48,320]{3,2,1,0:T(8,128)(2,1)S(1)} %maximum_select_fusion.1), channel_id=1, source_target_pairs={{0,96},{32,128},{64,160},{96,192},{128,224},{160,0},{192,32},{224,... | collective-permute-start | bytes 368648 | tf_op jit(solution)/shard_map/ppermute | solution.py:82
  31.7 22.2 %collective-permute-start.5 = (bf16[2,2,48,320]{3,2,1,0:T(8,128)(2,1)S(1)}, bf16[2,2,48,320]{3,2,1,0:T(8,128)(2,1)S(1)}, u32[]{:S(2)}, u32[]{:S(2)}) collective-permute-start(bf16[2,2,48,320]{3,2,1,0:T(8,128)(2,1)S(1)} %maximum_select_fusion.1), channel_id=1, source_target_pairs={{0,128},{32,160},{64,192},{96,224},{128,0},{160,32},{192,64},{224,... | collective-permute-start | bytes 368648 | tf_op jit(solution)/shard_map/ppermute | solution.py:82
  33.1 20.8 %collective-permute-start.6 = (bf16[2,2,48,320]{3,2,1,0:T(8,128)(2,1)S(1)}, bf16[2,2,48,320]{3,2,1,0:T(8,128)(2,1)S(1)}, u32[]{:S(2)}, u32[]{:S(2)}) collective-permute-start(bf16[2,2,48,320]{3,2,1,0:T(8,128)(2,1)S(1)} %maximum_select_fusion.1), channel_id=1, source_target_pairs={{0,160},{32,192},{64,224},{96,0},{128,32},{160,64},{192,96},{224,1... | collective-permute-start | bytes 368648 | tf_op jit(solution)/shard_map/ppermute | solution.py:82
  36.2 23.7 %collective-permute-start.7 = (bf16[2,2,48,320]{3,2,1,0:T(8,128)(2,1)S(1)}, bf16[2,2,48,320]{3,2,1,0:T(8,128)(2,1)S(1)}, u32[]{:S(2)}, u32[]{:S(2)}) collective-permute-start(bf16[2,2,48,320]{3,2,1,0:T(8,128)(2,1)S(1)} %maximum_select_fusion.1), channel_id=1, source_target_pairs={{0,192},{32,224},{64,0},{96,32},{128,64},{160,96},{192,128},{224,1... | collective-permute-start | bytes 368648 | tf_op jit(solution)/shard_map/ppermute | solution.py:82
  40.0 21.4 %collective-permute-start.8 = (bf16[2,2,48,320]{3,2,1,0:T(8,128)(2,1)S(1)}, bf16[2,2,48,320]{3,2,1,0:T(8,128)(2,1)S(1)}, u32[]{:S(2)}, u32[]{:S(2)}) collective-permute-start(bf16[2,2,48,320]{3,2,1,0:T(8,128)(2,1)S(1)} %maximum_select_fusion.1), channel_id=1, source_target_pairs={{0,224},{32,0},{64,32},{96,64},{128,96},{160,128},{192,160},{224,1... | collective-permute-start | bytes 368648 | tf_op jit(solution)/shard_map/ppermute | solution.py:82
  62.6 3.7 %copy-start.1 = (bf16[520,1536]{0,1:T(8,128)(2,1)S(1)}, bf16[520,1536]{0,1:T(8,128)(2,1)}, u32[]{:S(2)}) copy-start(bf16[520,1536]{0,1:T(8,128)(2,1)} %all-gather.2.cloned.1.call-done) | copy-start | bytes 4792324
  67.6 1.1 copy-start.4
  67.6 1.1 copy-start.3
  67.6 1.6 collective-permute-start.9
  76.2 27.3 %copy-start.2 = (bf16[512,192]{0,1:T(8,128)(2,1)S(1)}, bf16[512,192]{0,1:T(8,128)(2,1)}, u32[]{:S(2)}) copy-start(bf16[512,192]{0,1:T(8,128)(2,1)} %param.17) | copy-start | bytes 589828
  103.2 0.7 copy-start.8
  103.2 1.0 copy-start.5
  123.1 5.2 %copy-start.6 = (f32[512,8]{0,1:T(8,128)S(1)}, f32[512,8]{0,1:T(8,128)}, u32[]{:S(2)}) copy-start(f32[512,8]{0,1:T(8,128)} %param.26) | copy-start | bytes 49156
  123.1 5.2 %copy-start.7 = (s32[512,8]{0,1:T(8,128)S(1)}, s32[512,8]{0,1:T(8,128)}, u32[]{:S(2)}) copy-start(s32[512,8]{0,1:T(8,128)} %param.25) | copy-start | bytes 49156
  124.4 24.4 %all-to-all-start.1 = ((bf16[8,512,192]{1,2,0:T(8,128)(2,1)}), bf16[8,512,192]{1,2,0:T(8,128)(2,1)S(1)}, u32[]{:S(2)}, u32[]{:S(2)}) async-start(bf16[8,512,192]{1,2,0:T(8,128)(2,1)} %stack.111), calls=%async_computation.1 | async-start | bytes 3145728 | tf_op jit(solution)/shard_map/all_to_all | solution.py:192
  149.2 8.3 %copy-start.9 = (bf16[5,256,1536]{2,1,0:T(8,128)(2,1)S(1)}, bf16[5,256,1536]{2,1,0:T(8,128)(2,1)}, u32[]{:S(2)}) copy-start(bf16[5,256,1536]{2,1,0:T(8,128)(2,1)} %param.28) | copy-start | bytes 11796484
  162.6 24.9 %all-to-all-start.3 = ((bf16[8,512,192]{1,2,0:T(8,128)(2,1)}), bf16[8,512,192]{1,2,0:T(8,128)(2,1)S(1)}, u32[]{:S(2)}, u32[]{:S(2)}) async-start(bf16[8,512,192]{1,2,0:T(8,128)(2,1)} %bitcast.44), calls=%async_computation.3 | async-start | bytes 3145728 | tf_op jit(solution)/shard_map/all_to_all | solution.py:204
Sparse Core Ops, SparseCore 0:
  11.5 46.7 all-gather.1
